TPU v7x, 32 devices: a whole 2x2x4 slice. The times are simulated.
32 devices in a mesh: tile: 8 (over z, x), chan: 4 (over y, core).
Axes of the slice: x: 2, y: 2, z: 4, core: 2. Of those that a mesh axis runs over, the one named last changes fastest.
Arguments:
- visibility: bfloat16 [128, 2, 8, 512], P('tile', None, 'chan'), may hold values from -6 to 6
- imaging_weight: bfloat16 [128, 8, 512], P('tile', 'chan'), may hold values from 0.19921875 to 5
- position: int32 [128, 2, 512], P('tile'), may hold values from 0 to 3615
- anchor: int32 [128, 2], P('tile'), may hold values from 0 to 128
- destination: int32 [128], P('tile'), may hold values from 0 to 7, as said below
- block_count: int32 [8], P('tile'), may hold values from 12 to 16, as said below
- kernel: float32 [32, 16], replicated, may hold values from 0.25 to 1.5
Outputs:
- combined_grid: float32 [2, 2048, 256], P(None, ('tile', 'chan'))
- residual: bfloat16 [128, 2, 8, 512], P('tile', None, 'chan')
Inputs may be any that keep to these rules, and one draw needn't show every extreme that they name: `destination`: among each owner's 16 blocks at most 4 name one tile; one tile is named by exactly 4 blocks of every owner, all of them among that owner's first 8 blocks. Owner i's live blocks are its first block_count[i]; some owner has all 16 live. `position`: every entry is below 2^12. A program may carry positions, corners and other integer fields packed into fewer bits when they are sent, as long as nothing is lost.
All inputs are finite; a program needn't handle non-finite values.
Results may differ from a plain program's by a relative error of at most 0.009.
Values may be sent and summed in bfloat16 or wider, within the bound.
No kernel may reach another device: no remote copies, remote signals or barrier semaphores. Data moves between devices by JAX's collectives and lax.ppermute only.
A program may use at most 64 MiB of HBM per device.

v0:
```python
import functools

import jax
import jax.numpy as jnp
from jax import lax
from jax.experimental import pallas as pl
from jax.experimental.pallas import tpu as pltpu
from jax.sharding import PartitionSpec as P

TAPS = 16
OS = 32
SUB = 128
TS = 256
GROUP = 16
WINDOW = SUB + GROUP


def from_partner(block, axis, apart):
    count = lax.axis_size(axis)
    route = []
    for low in range(count):
        high = low | 1 << apart
        if high != low and high < count:
            route += [(low, high), (high, low)]
    return lax.ppermute(block, axis, route)


def build_taps(tv, base, out_ref, flip, origin):
    rows_out, width = out_ref.shape
    if flip:
        base = TS - TAPS - base
    base = base - origin
    low_bits = base & (GROUP - 1)
    group_of = base >> 4
    rows = lax.broadcasted_iota(jnp.int32, (GROUP, width), 0)
    reach = rows - low_bits
    wrapped = reach & (GROUP - 1)
    index = TAPS - 1 - wrapped if flip else wrapped
    level = [tv[tap : tap + 1, :] for tap in range(TAPS)]
    bit = 1
    while len(level) > 1:
        upper_half = (index & bit) != 0
        level = [jnp.where(upper_half, level[k + 1], level[k]) for k in range(0, len(level), 2)]
        bit *= 2
    spread = level[0]
    placed = group_of + (reach < 0).astype(jnp.int32)
    for part in range(rows_out // GROUP):
        out_ref[pl.ds(part * GROUP, GROUP), :] = jnp.where(placed == part, spread, 0.0)


def item_fields(got_ref, table_ref, item, channels):
    fields = got_ref[item].astype(jnp.float32)
    width = fields.shape[1]
    lanes = lax.broadcasted_iota(jnp.int32, (OS, width), 0)
    table = table_ref[...]
    taps = []
    bases = []
    for axis in range(2):
        offset = fields[3 * channels + 2 + axis : 3 * channels + 3 + axis].astype(jnp.int32)
        chosen = (lanes == offset).astype(jnp.bfloat16)
        taps.append(jnp.dot(table, chosen, preferred_element_type=jnp.float32))
        bases.append(fields[3 * channels + axis : 3 * channels + 1 + axis].astype(jnp.int32))
    return fields, taps, bases


def grid_kernel(flip, first, flags_ref, table_ref, got_ref, *rest):
    if first:
        acc_ref, row_ref, col_ref = rest
        acc_ref[...] = jnp.zeros(acc_ref.shape, jnp.float32)
    else:
        acc_in_ref, sum_ref, sym_ref, acc_ref, row_ref, col_ref = rest
        acc_ref[...] = acc_in_ref[...]
    items = got_ref.shape[0]
    channels = acc_ref.shape[1]

    def body(item, carry):
        @pl.when(flags_ref[0, item] != 0)
        def _():
            origin = pl.multiple_of(flags_ref[1, item], GROUP)
            fields, taps, bases = item_fields(got_ref, table_ref, item, channels)
            build_taps(taps[0], bases[0], row_ref, flip, origin)
            build_taps(taps[1], bases[1], col_ref, flip, 0)
            window = row_ref.shape[0]
            row_taps = row_ref[...].astype(jnp.bfloat16)
            col_taps = col_ref[...]
            for part in range(2):
                for chan in range(channels):
                    row = part * channels + chan
                    scale = fields[row : row + 1] * fields[2 * channels + chan : 2 * channels + chan + 1]
                    if flip and part == 1:
                        scale = -scale
                    weighted = (scale * col_taps).astype(jnp.bfloat16)
                    acc_ref[part, chan, pl.ds(origin, window), :] += lax.dot_general(
                        row_taps,
                        weighted,
                        (((1,), (1,)), ((), ())),
                        preferred_element_type=jnp.float32,
                    )

        return carry

    lax.fori_loop(0, items, body, 0)
    if not first:
        for part in range(2):
            total = acc_ref[part, 0]
            sym_ref[part, 0] = total.astype(jnp.bfloat16)
            for chan in range(1, channels):
                layer = acc_ref[part, chan]
                sym_ref[part, chan] = layer.astype(jnp.bfloat16)
                total = total + layer
            sum_ref[part] = total


def degrid_kernel(flags_ref, table_ref, got_ref, sym_ref, out_ref, row_ref, col_ref):
    items = got_ref.shape[0]
    channels = sym_ref.shape[1]
    out_ref[...] = jnp.zeros(out_ref.shape, out_ref.dtype)

    def body(item, carry):
        @pl.when(flags_ref[0, item] != 0)
        def _():
            origin = pl.multiple_of(flags_ref[1, item], GROUP)
            _, taps, bases = item_fields(got_ref, table_ref, item, channels)
            build_taps(taps[0], bases[0], row_ref, False, origin)
            build_taps(taps[1], bases[1], col_ref, False, 0)
            window = row_ref.shape[0]
            col_taps = col_ref[...].astype(jnp.bfloat16)
            row_taps = row_ref[...]
            norm = 1.0 / (TAPS * TAPS)
            for part in range(2):
                rows = []
                for chan in range(channels):
                    inner = jnp.dot(
                        sym_ref[part, chan, pl.ds(origin, window), :],
                        col_taps,
                        preferred_element_type=jnp.float32,
                    )
                    rows.append(jnp.sum(row_taps * inner, axis=0, keepdims=True) * norm)
                out_ref[item, part] = jnp.concatenate(rows, axis=0).astype(out_ref.dtype)

        return carry

    lax.fori_loop(0, items, body, 0)


def run_grid(flags, table, got, channels, flip, acc_in=None):
    width = got.shape[2]
    vmem = pltpu.VMEM
    acc_shape = (2, channels, TS, TS)
    taps_scratch = [vmem((WINDOW, width), jnp.float32), vmem((TS, width), jnp.float32)]
    first = acc_in is None
    if first:
        out_shape = jax.ShapeDtypeStruct(acc_shape, jnp.float32)
        out_specs = pl.BlockSpec(memory_space=vmem)
        scratch = taps_scratch
        operands = (flags, table, got)
    else:
        out_shape = (
            jax.ShapeDtypeStruct((2, TS, TS), jnp.float32),
            jax.ShapeDtypeStruct(acc_shape, jnp.bfloat16),
        )
        out_specs = (pl.BlockSpec(memory_space=vmem), pl.BlockSpec(memory_space=vmem))
        scratch = [vmem(acc_shape, jnp.float32)] + taps_scratch
        operands = (flags, table, got, acc_in)
    return pl.pallas_call(
        functools.partial(grid_kernel, flip, first),
        out_shape=out_shape,
        in_specs=[pl.BlockSpec(memory_space=pltpu.SMEM)]
        + [pl.BlockSpec(memory_space=vmem) for _ in operands[1:]],
        out_specs=out_specs,
        scratch_shapes=scratch,
    )(*operands)


def run_degrid(flags, table, got, sym):
    items, _, width = got.shape
    channels = sym.shape[1]
    vmem = pltpu.VMEM
    return pl.pallas_call(
        degrid_kernel,
        out_shape=jax.ShapeDtypeStruct((items, 2, channels, width), jnp.bfloat16),
        in_specs=[pl.BlockSpec(memory_space=pltpu.SMEM)]
        + [pl.BlockSpec(memory_space=vmem) for _ in range(3)],
        out_specs=pl.BlockSpec(memory_space=vmem),
        scratch_shapes=[vmem((WINDOW, width), jnp.float32), vmem((TS, width), jnp.float32)],
    )(flags, table, got, sym)


def slot_flags(got, channels, mirrored):
    live = got[:, 3 * channels + 4, 0] > 0
    row_base = got[:, 3 * channels].astype(jnp.int32)
    if mirrored:
        lowest = TS - TAPS - jnp.max(row_base, axis=1)
    else:
        lowest = jnp.min(row_base, axis=1)
    origin = jnp.minimum(lowest // GROUP * GROUP, TS - WINDOW)
    return jnp.stack([live.astype(jnp.int32), origin])


def per_device(visibility, imaging_weight, position, anchor, destination, block_count, kernel):
    tile_count = lax.axis_size("tile")
    mirror_bit = tile_count.bit_length() - 2
    owned_blocks, _, channels, block_width = visibility.shape
    bucket = max(2, 2 * owned_blocks // tile_count)
    slot_total = tile_count * bucket
    block_ids = jnp.arange(owned_blocks, dtype=jnp.int32)
    is_live = block_ids < block_count[0]
    same_tile = destination[:, None] == destination[None, :]
    earlier = block_ids[None, :] < block_ids[:, None]
    rank_in_tile = jnp.sum((same_tile & earlier).astype(jnp.int32), axis=1)
    slot_of = destination * bucket + rank_in_tile

    base = anchor[:, :, None] + position // OS
    offset = position % OS
    live_row = jnp.broadcast_to(is_live[:, None, None], (owned_blocks, 1, block_width))
    packed = jnp.concatenate(
        [
            visibility[:, 0],
            visibility[:, 1],
            imaging_weight,
            base.astype(jnp.bfloat16),
            offset.astype(jnp.bfloat16),
            live_row.astype(jnp.bfloat16),
        ],
        axis=1,
    )
    slot_ids = jnp.arange(slot_total, dtype=jnp.int32)
    matches = slot_of[None, :] == slot_ids[:, None]
    filled = jnp.any(matches, axis=1)
    source = jnp.sum(jnp.where(matches, block_ids[None, :], 0), axis=1)
    send = jnp.where(filled[:, None, None], packed[source], jnp.zeros((), jnp.bfloat16))
    got_own = lax.all_to_all(send, "tile", split_axis=0, concat_axis=0, tiled=True)
    got_other = from_partner(got_own, "tile", mirror_bit)
    table = kernel.T.astype(jnp.bfloat16)

    own_flags = slot_flags(got_own, channels, False)
    partial_grid = run_grid(own_flags, table, got_own, channels, False)
    other_flags = slot_flags(got_other, channels, True)
    grid_sum, symmetric = run_grid(other_flags, table, got_other, channels, True, partial_grid)
    combined_grid = lax.psum_scatter(grid_sum, "chan", scatter_dimension=1, tiled=True)
    own_results = run_degrid(own_flags, table, got_own, symmetric)
    returned_slots = lax.all_to_all(own_results, "tile", split_axis=0, concat_axis=0, tiled=True)
    returned = jnp.where(
        is_live[:, None, None, None], returned_slots[slot_of], jnp.zeros((), jnp.bfloat16)
    )
    residual = (visibility.astype(jnp.float32) - returned.astype(jnp.float32)).astype(jnp.bfloat16)
    return (combined_grid, residual)


def solution(mesh):
    placed = (
        P("tile", None, "chan", None),
        P("tile", "chan", None),
        P("tile", None, None),
        P("tile", None),
        P("tile"),
        P("tile"),
        P(),
    )
    return jax.shard_map(
        per_device,
        mesh=mesh,
        in_specs=placed,
        out_specs=(P(None, ("tile", "chan"), None), P("tile", None, "chan", None)),
        check_vma=False,
    )
```

profile of v0, /device:TPU:0, one launch (start us, length us, event | category | flops | bytes accessed | tf_op | source)
XLA Modules:
  0.0 111.8 jit_solution(3043610073108313128)
XLA Ops:
  7.2 0.9 convert_reduce_fusion
  8.1 0.1 select_reduce_fusion
  8.2 0.1 fusion.5
  8.3 0.6 copy-done.6
  8.9 0.1 copy.17
  9.0 0.9 slice_bitcast_fusion
  10.5 0.3 fusion.2
  10.8 0.1 broadcast_in_dim.57
  10.9 0.7 copy-done.4
  11.6 0.3 concatenate.3
  11.9 0.6 gather_fusion
  12.5 0.9 broadcast_select_fusion
  13.4 7.4 %all-to-all-start = ((bf16[32,11,512]{2,1,0:T(8,128)(2,1)}), bf16[32,11,512]{2,1,0:T(8,128)(2,1)S(1)}, u32[]{:S(2)}, u32[]{:S(2)}) async-start(bf16[32,11,512]{2,1,0:T(8,128)(2,1)} %broadcast_select_fusion), calls=%async_computation | async-start | bytes 1048576 | tf_op jit(solution)/shard_map/all_to_all | solution.py:232
  20.8 0.0 reduce-scatter.2.cloned.1.call-start
  20.8 0.6 convert_bitcast_fusion.table_ref
  21.4 13.8 %all-to-all-done.got_ref = bf16[32,11,512]{2,1,0:T(8,128)(2,1)S(1)} async-done(((bf16[32,11,512]{2,1,0:T(8,128)(2,1)}), bf16[32,11,512]{2,1,0:T(8,128)(2,1)S(1)}, u32[]{:S(2)}, u32[]{:S(2)}) %all-to-all-start) | async-done | bytes 360480 | tf_op jit(solution)/shard_map/all_to_all | solution.py:232
  35.3 0.7 fusion
  35.9 0.2 collective-permute-start
  36.2 0.7 fusion.4
  36.8 0.6 pad_add_fusion.1.flags_ref
  37.4 7.2 %shard_map.86.rest_0_ = f32[2,2,256,256]{3,2,1,0:T(8,128)} custom-call(s32[2,32]{1,0:T(2,128)} %pad_add_fusion.1.flags_ref, bf16[16,32]{1,0:T(8,128)(2,1)} %convert_bitcast_fusion.table_ref, bf16[32,11,512]{2,1,0:T(8,128)(2,1)} %copy-done), custom_call_target="tpu_custom_call" | custom-call | tf_op jit(solution)/shard_map/pallas_call | solution.py:165
  44.6 15.0 %collective-permute-done.got_ref = bf16[32,11,512]{2,1,0:T(8,128)(2,1)S(1)} collective-permute-done((bf16[32,11,512]{2,1,0:T(8,128)(2,1)S(1)}, bf16[32,11,512]{2,1,0:T(8,128)(2,1)S(1)}, u32[]{:S(2)}, u32[]{:S(2)}) %collective-permute-start) | collective-permute-done | bytes 360480 | tf_op jit(solution)/shard_map/ppermute | solution.py:25
  59.6 0.7 fusion.1
  60.3 0.7 fusion.3
  61.0 0.6 pad_add_fusion.flags_ref
  61.6 24.3 %shard_map.87 = (f32[2,256,256]{2,1,0:T(8,128)}, bf16[2,2,256,256]{3,2,1,0:T(8,128)(2,1)}) custom-call(s32[2,32]{1,0:T(2,128)} %pad_add_fusion.flags_ref, bf16[16,32]{1,0:T(8,128)(2,1)} %convert_bitcast_fusion.table_ref, bf16[32,11,512]{2,1,0:T(8,128)(2,1)} %copy-done.1, f32[2,2,256,256]{3,2,1,0:T(8,128)} %shard_map.86.rest_0_), custom_call_target="tpu_custom_call" | custom-call | tf_op jit(solution)/shard_map/pallas_call | solution.py:165
  85.9 6.2 %shard_map.88 = bf16[32,2,2,512]{3,2,1,0:T(2,128)(2,1)} custom-call(s32[2,32]{1,0:T(2,128)} %pad_add_fusion.1.flags_ref, bf16[16,32]{1,0:T(8,128)(2,1)} %convert_bitcast_fusion.table_ref, bf16[32,11,512]{2,1,0:T(8,128)(2,1)} %copy-done, bf16[2,2,256,256]{3,2,1,0:T(8,128)(2,1)} %get-tuple-element.5.sym_ref), custom_call_target="tpu_custom_call" | custom-call | tf_op jit(solution)/shard_map/pallas_call | solution.py:179
  92.1 3.4 %all-to-all-start.1 = ((bf16[32,2,2,512]{3,2,1,0:T(2,128)(2,1)}), bf16[32,2,2,512]{3,2,1,0:T(2,128)(2,1)S(1)}, u32[]{:S(2)}, u32[]{:S(2)}) async-start(bf16[32,2,2,512]{3,2,1,0:T(2,128)(2,1)} %shard_map.88), calls=%async_computation.2 | async-start | bytes 262144 | tf_op jit(solution)/shard_map/all_to_all | solution.py:242
  95.5 7.4 %all-to-all-done.1 = bf16[32,2,2,512]{3,2,1,0:T(2,128)(2,1)S(1)} async-done(((bf16[32,2,2,512]{3,2,1,0:T(2,128)(2,1)}), bf16[32,2,2,512]{3,2,1,0:T(2,128)(2,1)S(1)}, u32[]{:S(2)}, u32[]{:S(2)}) %all-to-all-start.1) | async-done | bytes 131104 | tf_op jit(solution)/shard_map/all_to_all | solution.py:242
  102.9 0.7 gather_fusion.1
  103.6 0.8 subtract_convert_fusion
  104.3 0.6 reduce-scatter.2.cloned.1.call-done
  (23 shorter events, 0.1 us)
Async XLA Ops:
  7.2 0.9 copy-start.7
  8.2 0.7 copy-start.6
  9.0 1.5 %copy-start.3 = (s32[16,2,512]{2,1,0:T(2,128)S(1)}, s32[16,2,512]{2,1,0:T(2,128)}, u32[]{:S(2)}) copy-start(s32[16,2,512]{2,1,0:T(2,128)} %param.9) | copy-start | bytes 196612
  10.8 0.8 copy-start.4
  13.4 7.5 %copy-start.5 = (f32[32,16]{0,1:T(8,128)S(1)}, f32[32,16]{0,1:T(8,128)}, u32[]{:S(2)}) copy-start(f32[32,16]{0,1:T(8,128)} %param.13) | copy-start | bytes 6148
  13.4 21.9 %all-to-all-start = ((bf16[32,11,512]{2,1,0:T(8,128)(2,1)}), bf16[32,11,512]{2,1,0:T(8,128)(2,1)S(1)}, u32[]{:S(2)}, u32[]{:S(2)}) async-start(bf16[32,11,512]{2,1,0:T(8,128)(2,1)} %broadcast_select_fusion), calls=%async_computation | async-start | bytes 1048576 | tf_op jit(solution)/shard_map/all_to_all | solution.py:232
  20.8 84.2 %reduce-scatter.2.cloned.1.call-start = ((), (), s32[]{:S(2)}) async-start(), calls=%async_computation.3 | async-start | bytes 655360 | tf_op jit(solution)/shard_map/reduce_scatter | solution.py:240
  35.3 2.2 %copy-start = (bf16[32,11,512]{2,1,0:T(8,128)(2,1)}, bf16[32,11,512]{2,1,0:T(8,128)(2,1)S(1)}, u32[]{:S(2)}) copy-start(bf16[32,11,512]{2,1,0:T(8,128)(2,1)S(1)} %all-to-all-done.got_ref) | copy-start | bytes 1081348
  35.9 23.7 %collective-permute-start = (bf16[32,11,512]{2,1,0:T(8,128)(2,1)S(1)}, bf16[32,11,512]{2,1,0:T(8,128)(2,1)S(1)}, u32[]{:S(2)}, u32[]{:S(2)}) collective-permute-start(bf16[32,11,512]{2,1,0:T(8,128)(2,1)S(1)} %all-to-all-done.got_ref), channel_id=1, source_target_pairs={{0,16},{16,0},{4,20},{20,4},{8,24},{24,8},{12,28},{28,12},{1,17},{... | collective-permute-start | bytes 1081352 | tf_op jit(solution)/shard_map/ppermute | solution.py:25
  59.6 1.9 %copy-start.1 = (bf16[32,11,512]{2,1,0:T(8,128)(2,1)}, bf16[32,11,512]{2,1,0:T(8,128)(2,1)S(1)}, u32[]{:S(2)}) copy-start(bf16[32,11,512]{2,1,0:T(8,128)(2,1)S(1)} %collective-permute-done.got_ref) | copy-start | bytes 1081348
  92.1 10.8 %all-to-all-start.1 = ((bf16[32,2,2,512]{3,2,1,0:T(2,128)(2,1)}), bf16[32,2,2,512]{3,2,1,0:T(2,128)(2,1)S(1)}, u32[]{:S(2)}, u32[]{:S(2)}) async-start(bf16[32,2,2,512]{3,2,1,0:T(2,128)(2,1)} %shard_map.88), calls=%async_computation.2 | async-start | bytes 262144 | tf_op jit(solution)/shard_map/all_to_all | solution.py:242
  95.5 8.1 %copy-start.2 = (bf16[16,2,2,512]{3,2,1,0:T(2,128)(2,1)S(1)}, bf16[16,2,2,512]{3,2,1,0:T(2,128)(2,1)}, u32[]{:S(2)}) copy-start(bf16[16,2,2,512]{3,2,1,0:T(2,128)(2,1)} %param.7) | copy-start | bytes 196612
Sparse Core Ops, SparseCore 0:
  86.0 18.9 reduce-scatter.1
where the time goes:
time: 114 us; the launch traced here: 112 us
  Pallas kernels  37.7 us (33%)
  waiting for transfers between devices  36.8 us (32%)
  between operations  14.8 us (13%)
  starting transfers between devices  11 us (10%)
  other arithmetic  7.58 us (7%)
  local copies, waits for them, and re-layouts  3.85 us (3%)
    pallas_call x2, Pallas kernels, run_grid(): pl.pallas_call(functools.partial(grid_kernel, flip, first), out_shape=out...  31.5 us
    ppermute x1, waiting for transfers between devices, from_partner(): return lax.ppermute(block, axis, route)  15 us
    all_to_all x1, waiting for transfers between devices, per_device(): lax.all_to_all(send, 'tile', split_axis=0, concat_axis=0, tiled=True)  13.8 us
    all_to_all x1, starting transfers between devices, per_device(): lax.all_to_all(send, 'tile', split_axis=0, concat_axis=0, tiled=True)  7.41 us
    all_to_all x1, waiting for transfers between devices, per_device(): lax.all_to_all(own_results, 'tile', split_axis=0, concat_axis=0, tiled=True)  7.37 us
    pallas_call x1, Pallas kernels, run_degrid(): pl.pallas_call(degrid_kernel, out_shape=jax.ShapeDtypeStruct((items, 2, c...  6.2 us
    all_to_all x1, starting transfers between devices, per_device(): lax.all_to_all(own_results, 'tile', split_axis=0, concat_axis=0, tiled=True)  3.37 us
  transfers between devices with their start and end apart: 4, of which 4 were waited for; matrix products, arithmetic and copies ran while one was open for 3% of the time, Pallas kernels for 12%

commit v1 on v0

--- a/solution.py
+++ b/solution.py
@@ -99,7 +99,7 @@
 
         return carry
 
-    lax.fori_loop(0, items, body, 0)
+    lax.fori_loop(0, items, body, 0, unroll=2)
     if not first:
         for part in range(2):
             total = acc_ref[part, 0]
@@ -140,7 +140,7 @@
 
         return carry
 
-    lax.fori_loop(0, items, body, 0)
+    lax.fori_loop(0, items, body, 0, unroll=2)
 
 
 def run_grid(flags, table, got, channels, flip, acc_in=None):

time: 114 us -> 114 us (level); the launches traced: 112 us -> 113 us
  starting transfers between devices: 11 us -> 25.6 us
  Pallas kernels: 37.7 us -> 26.1 us
  waiting for transfers between devices: 36.8 us -> 35.5 us
    all_to_all x1, starting transfers between devices: 3.37 us -> 17.9 us  [per_device(): lax.all_to_all(own_results, 'tile', split_axis=0, concat_axis=0, tiled=True)]
    pallas_call x2, Pallas kernels: 31.5 us -> 18 us  [run_grid(): pl.pallas_call(functools.partial(grid_kernel, flip, first), out_shape=out...]
    ppermute x1, waiting for transfers between devices: 15 us -> 12.4 us  [from_partner(): return lax.ppermute(block, axis, route)]
    pallas_call x1, Pallas kernels: 6.2 us -> 8.08 us  [run_degrid(): pl.pallas_call(degrid_kernel, out_shape=jax.ShapeDtypeStruct((items, 2, c...]
    reduce_scatter x1, waiting for transfers between devices: 0.63 us -> 1.95 us  [per_device(): lax.psum_scatter(grid_sum, 'chan', scatter_dimension=1, tiled=True)]
  transfers between devices with their start and end apart: 4 -> 4, of which waited for: 4 -> 4; matrix products, arithmetic and copies ran while one was open for 3% -> 3% of each run, Pallas kernels for 12% -> 16%
where the time goes in v1:
time: 114 us; the launch traced here: 113 us
  waiting for transfers between devices  35.5 us (31%)
  Pallas kernels  26.1 us (23%)
  starting transfers between devices  25.6 us (22%)
  between operations  14.8 us (13%)
  other arithmetic  7.58 us (7%)
  local copies, waits for them, and re-layouts  3.84 us (3%)
    pallas_call x2, Pallas kernels, run_grid(): pl.pallas_call(functools.partial(grid_kernel, flip, first), out_shape=out...  18 us
    all_to_all x1, starting transfers between devices, per_device(): lax.all_to_all(own_results, 'tile', split_axis=0, concat_axis=0, tiled=True)  17.9 us
    all_to_all x1, waiting for transfers between devices, per_device(): lax.all_to_all(send, 'tile', split_axis=0, concat_axis=0, tiled=True)  13.8 us
    ppermute x1, waiting for transfers between devices, from_partner(): return lax.ppermute(block, axis, route)  12.4 us
    pallas_call x1, Pallas kernels, run_degrid(): pl.pallas_call(degrid_kernel, out_shape=jax.ShapeDtypeStruct((items, 2, c...  8.08 us
    all_to_all x1, starting transfers between devices, per_device(): lax.all_to_all(send, 'tile', split_axis=0, concat_axis=0, tiled=True)  7.41 us
    all_to_all x1, waiting for transfers between devices, per_device(): lax.all_to_all(own_results, 'tile', split_axis=0, concat_axis=0, tiled=True)  7.31 us
  transfers between devices with their start and end apart: 4, of which 4 were waited for; matrix products, arithmetic and copies ran while one was open for 3% of the time, Pallas kernels for 16%

profile of v1, /device:TPU:0, one launch (start us, length us, event | category | flops | bytes accessed | tf_op | source)
XLA Modules:
  0.0 113.5 jit_solution(7832604602206041055)
XLA Ops:
  7.2 0.9 convert_reduce_fusion
  8.1 0.1 select_reduce_fusion
  8.2 0.1 fusion.5
  8.3 0.6 copy-done.6
  8.9 0.1 copy.17
  9.0 0.9 slice_bitcast_fusion
  10.5 0.3 fusion.2
  10.8 0.1 broadcast_in_dim.57
  10.9 0.7 copy-done.4
  11.6 0.3 concatenate.3
  11.9 0.6 gather_fusion
  12.5 0.9 broadcast_select_fusion
  13.4 7.4 %all-to-all-start = ((bf16[32,11,512]{2,1,0:T(8,128)(2,1)}), bf16[32,11,512]{2,1,0:T(8,128)(2,1)S(1)}, u32[]{:S(2)}, u32[]{:S(2)}) async-start(bf16[32,11,512]{2,1,0:T(8,128)(2,1)} %broadcast_select_fusion), calls=%async_computation | async-start | bytes 1048576 | tf_op jit(solution)/shard_map/all_to_all | solution.py:232
  20.8 0.0 reduce-scatter.2.cloned.1.call-start
  20.8 0.6 convert_bitcast_fusion.table_ref
  21.4 13.8 %all-to-all-done.got_ref = bf16[32,11,512]{2,1,0:T(8,128)(2,1)S(1)} async-done(((bf16[32,11,512]{2,1,0:T(8,128)(2,1)}), bf16[32,11,512]{2,1,0:T(8,128)(2,1)S(1)}, u32[]{:S(2)}, u32[]{:S(2)}) %all-to-all-start) | async-done | bytes 360480 | tf_op jit(solution)/shard_map/all_to_all | solution.py:232
  35.3 0.7 fusion
  35.9 0.2 collective-permute-start
  36.2 0.7 fusion.4
  36.8 0.6 pad_add_fusion.1.flags_ref
  37.4 9.8 %shard_map.86.rest_0_ = f32[2,2,256,256]{3,2,1,0:T(8,128)} custom-call(s32[2,32]{1,0:T(2,128)} %pad_add_fusion.1.flags_ref, bf16[16,32]{1,0:T(8,128)(2,1)} %convert_bitcast_fusion.table_ref, bf16[32,11,512]{2,1,0:T(8,128)(2,1)} %copy-done), custom_call_target="tpu_custom_call" | custom-call | tf_op jit(solution)/shard_map/pallas_call | solution.py:165
  47.2 12.4 %collective-permute-done.got_ref = bf16[32,11,512]{2,1,0:T(8,128)(2,1)S(1)} collective-permute-done((bf16[32,11,512]{2,1,0:T(8,128)(2,1)S(1)}, bf16[32,11,512]{2,1,0:T(8,128)(2,1)S(1)}, u32[]{:S(2)}, u32[]{:S(2)}) %collective-permute-start) | collective-permute-done | bytes 360480 | tf_op jit(solution)/shard_map/ppermute | solution.py:25
  59.6 0.7 fusion.1
  60.3 0.7 fusion.3
  61.0 0.6 pad_add_fusion.flags_ref
  61.6 8.2 %shard_map.87 = (f32[2,256,256]{2,1,0:T(8,128)}, bf16[2,2,256,256]{3,2,1,0:T(8,128)(2,1)}) custom-call(s32[2,32]{1,0:T(2,128)} %pad_add_fusion.flags_ref, bf16[16,32]{1,0:T(8,128)(2,1)} %convert_bitcast_fusion.table_ref, bf16[32,11,512]{2,1,0:T(8,128)(2,1)} %copy-done.1, f32[2,2,256,256]{3,2,1,0:T(8,128)} %shard_map.86.rest_0_), custom_call_target="tpu_custom_call" | custom-call | tf_op jit(solution)/shard_map/pallas_call | solution.py:165
  69.8 8.1 %shard_map.88 = bf16[32,2,2,512]{3,2,1,0:T(2,128)(2,1)} custom-call(s32[2,32]{1,0:T(2,128)} %pad_add_fusion.1.flags_ref, bf16[16,32]{1,0:T(8,128)(2,1)} %convert_bitcast_fusion.table_ref, bf16[32,11,512]{2,1,0:T(8,128)(2,1)} %copy-done, bf16[2,2,256,256]{3,2,1,0:T(8,128)(2,1)} %get-tuple-element.5.sym_ref), custom_call_target="tpu_custom_call" | custom-call | tf_op jit(solution)/shard_map/pallas_call | solution.py:179
  77.9 17.9 %all-to-all-start.1 = ((bf16[32,2,2,512]{3,2,1,0:T(2,128)(2,1)}), bf16[32,2,2,512]{3,2,1,0:T(2,128)(2,1)S(1)}, u32[]{:S(2)}, u32[]{:S(2)}) async-start(bf16[32,2,2,512]{3,2,1,0:T(2,128)(2,1)} %shard_map.88), calls=%async_computation.2 | async-start | bytes 262144 | tf_op jit(solution)/shard_map/all_to_all | solution.py:242
  95.9 7.3 %all-to-all-done.1 = bf16[32,2,2,512]{3,2,1,0:T(2,128)(2,1)S(1)} async-done(((bf16[32,2,2,512]{3,2,1,0:T(2,128)(2,1)}), bf16[32,2,2,512]{3,2,1,0:T(2,128)(2,1)S(1)}, u32[]{:S(2)}, u32[]{:S(2)}) %all-to-all-start.1) | async-done | bytes 131104 | tf_op jit(solution)/shard_map/all_to_all | solution.py:242
  103.2 0.7 gather_fusion.1
  103.9 0.8 subtract_convert_fusion
  104.7 1.9 %reduce-scatter.2.cloned.1.call-done = f32[2,64,256]{2,1,0:T(8,128)} async-done(((f32[2,256,256]{2,1,0:T(8,128)}), f32[2,64,256]{2,1,0:T(8,128)}) %reduce-scatter.2.cloned.1.call-update) | async-done | bytes 131088 | tf_op jit(solution)/shard_map/reduce_scatter | solution.py:240
  (23 shorter events, 0.1 us)
Async XLA Ops:
  7.2 0.9 copy-start.7
  8.2 0.7 copy-start.6
  9.0 1.5 %copy-start.3 = (s32[16,2,512]{2,1,0:T(2,128)S(1)}, s32[16,2,512]{2,1,0:T(2,128)}, u32[]{:S(2)}) copy-start(s32[16,2,512]{2,1,0:T(2,128)} %param.9) | copy-start | bytes 196612
  10.8 0.8 copy-start.4
  13.4 7.5 %copy-start.5 = (f32[32,16]{0,1:T(8,128)S(1)}, f32[32,16]{0,1:T(8,128)}, u32[]{:S(2)}) copy-start(f32[32,16]{0,1:T(8,128)} %param.13) | copy-start | bytes 6148
  13.4 21.9 %all-to-all-start = ((bf16[32,11,512]{2,1,0:T(8,128)(2,1)}), bf16[32,11,512]{2,1,0:T(8,128)(2,1)S(1)}, u32[]{:S(2)}, u32[]{:S(2)}) async-start(bf16[32,11,512]{2,1,0:T(8,128)(2,1)} %broadcast_select_fusion), calls=%async_computation | async-start | bytes 1048576 | tf_op jit(solution)/shard_map/all_to_all | solution.py:232
  20.8 85.8 %reduce-scatter.2.cloned.1.call-start = ((), (), s32[]{:S(2)}) async-start(), calls=%async_computation.3 | async-start | bytes 655360 | tf_op jit(solution)/shard_map/reduce_scatter | solution.py:240
  35.3 2.2 %copy-start = (bf16[32,11,512]{2,1,0:T(8,128)(2,1)}, bf16[32,11,512]{2,1,0:T(8,128)(2,1)S(1)}, u32[]{:S(2)}) copy-start(bf16[32,11,512]{2,1,0:T(8,128)(2,1)S(1)} %all-to-all-done.got_ref) | copy-start | bytes 1081348
  35.9 23.7 %collective-permute-start = (bf16[32,11,512]{2,1,0:T(8,128)(2,1)S(1)}, bf16[32,11,512]{2,1,0:T(8,128)(2,1)S(1)}, u32[]{:S(2)}, u32[]{:S(2)}) collective-permute-start(bf16[32,11,512]{2,1,0:T(8,128)(2,1)S(1)} %all-to-all-done.got_ref), channel_id=1, source_target_pairs={{0,16},{16,0},{4,20},{20,4},{8,24},{24,8},{12,28},{28,12},{1,17},{... | collective-permute-start | bytes 1081352 | tf_op jit(solution)/shard_map/ppermute | solution.py:25
  59.6 1.9 %copy-start.1 = (bf16[32,11,512]{2,1,0:T(8,128)(2,1)}, bf16[32,11,512]{2,1,0:T(8,128)(2,1)S(1)}, u32[]{:S(2)}) copy-start(bf16[32,11,512]{2,1,0:T(8,128)(2,1)S(1)} %collective-permute-done.got_ref) | copy-start | bytes 1081348
  77.9 25.3 %all-to-all-start.1 = ((bf16[32,2,2,512]{3,2,1,0:T(2,128)(2,1)}), bf16[32,2,2,512]{3,2,1,0:T(2,128)(2,1)S(1)}, u32[]{:S(2)}, u32[]{:S(2)}) async-start(bf16[32,2,2,512]{3,2,1,0:T(2,128)(2,1)} %shard_map.88), calls=%async_computation.2 | async-start | bytes 262144 | tf_op jit(solution)/shard_map/all_to_all | solution.py:242
  95.9 8.0 %copy-start.2 = (bf16[16,2,2,512]{3,2,1,0:T(2,128)(2,1)S(1)}, bf16[16,2,2,512]{3,2,1,0:T(2,128)(2,1)}, u32[]{:S(2)}) copy-start(bf16[16,2,2,512]{3,2,1,0:T(2,128)(2,1)} %param.7) | copy-start | bytes 196612
Sparse Core Ops, SparseCore 0:
  69.9 36.6 reduce-scatter.1
